TPU v7x, 256 devices: a whole 4x4x8 slice. The times are simulated.
256 devices in a mesh: section: 16 (over z_lo, y, core), tensor: 16 (over x, z_hi).
Axes of the slice: x: 4, y: 4, z: 8 (z_hi: 4, z_lo: 2; z = z_hi * 2 + z_lo), core: 2. Of those that a mesh axis runs over, the one named last changes fastest.
Arguments:
- hidden: bfloat16 [16, 64, 8192], P('section'), may hold values from -14 to 14
- head: bfloat16 [8192, 65536], P('section', 'tensor'), may hold values from -0.25 to 0.25
- exit_loss_weight: float32 [16], P('section'), may hold values from 2 to 32
Outputs:
- grad_hidden: float32 [1024, 8192], P('tensor', 'section')
- grad_head: bfloat16 [8192, 65536], P('section', 'tensor')
All inputs are finite; a program needn't handle non-finite values.
Results may differ from a plain program's by a relative error of at most 0.011.
Values may be sent and summed in bfloat16 or wider, within the bound.
No kernel may reach another device: no remote copies, remote signals or barrier semaphores. Data moves between devices by JAX's collectives and lax.ppermute only.
A program may use at most 128 MiB of HBM per device.

v0:
```python
import jax
import jax.numpy as jnp
from jax import lax
from jax.sharding import PartitionSpec as P

scaling_divisor = 2.0


def from_root(value, axis, source):
    kept = jnp.where(lax.axis_index(axis) == source, value, 0).astype(value.dtype)
    return lax.psum(kept, axis)


def local(hidden, head, exit_loss_weight):
    departure_number = lax.axis_size("section")
    tok_count = hidden.shape[1]
    row_count = departure_number * tok_count
    local_cols = lax.all_to_all(hidden, "section", split_axis=2, concat_axis=0, tiled=True)
    flat_hidden = local_cols.reshape(row_count, local_cols.shape[2])
    own_logits = lax.psum_scatter(
        jnp.dot(flat_hidden, head, preferred_element_type=jnp.float32),
        "section",
        scatter_dimension=0,
        tiled=True,
    )
    mentor_score_matrix = from_root(own_logits, "section", departure_number - 1)
    mentor_distribution = mentor_score_matrix / scaling_divisor
    local_smax = jnp.max(own_logits, axis=1)
    local_tmax = jnp.max(mentor_distribution, axis=1)
    student_max, teacher_max = lax.pmax((local_smax, local_tmax), "tensor")
    student_sum, teacher_sum = lax.psum(
        (
            jnp.sum(jnp.exp(own_logits - student_max[:, None]), axis=1),
            jnp.sum(jnp.exp(mentor_distribution - teacher_max[:, None]), axis=1),
        ),
        "tensor",
    )
    student_norm = student_max + jnp.log(student_sum)
    teacher_norm = teacher_max + jnp.log(teacher_sum)
    log_student = own_logits - student_norm[:, None]
    log_teacher = mentor_distribution - teacher_norm[:, None]
    log_mixture = jnp.logaddexp(log_student, log_teacher) - jnp.log(2.0)
    midpoint_difference = 0.5 * (log_student - log_mixture)
    student = jnp.exp(log_student)
    average = lax.psum(jnp.sum(student * midpoint_difference, axis=1), "tensor")
    grad_logits = (exit_loss_weight[0] * student * (midpoint_difference - average[:, None])).astype(
        jnp.bfloat16
    )
    piece = lax.all_gather(grad_logits, "section", axis=0, tiled=True)
    head_grad = lax.dot_general(
        flat_hidden, piece, (((0,), (0,)), ((), ())), preferred_element_type=jnp.float32
    )
    row_grad = lax.dot_general(
        piece, head, (((1,), (1,)), ((), ())), preferred_element_type=jnp.float32
    )
    hidden_part = row_grad
    head_grad, hidden_part = (head_grad, hidden_part)
    grad_hidden = lax.psum_scatter(hidden_part, "tensor", scatter_dimension=0, tiled=True)
    return (grad_hidden, head_grad.astype(jnp.bfloat16))


def solution(mesh):
    placed = (P("section", None, None), P("section", "tensor"), P("section"))
    return jax.shard_map(
        local,
        mesh=mesh,
        in_specs=placed,
        out_specs=(P("tensor", "section"), P("section", "tensor")),
        check_vma=False,
    )
```

profile of v0, /device:TPU:8, one launch (start us, length us, event | category | flops | bytes accessed | tf_op | source)
XLA Modules:
  0.0 624.9 jit_solution(6586606897295019781)
XLA Ops:
  7.2 9.2 %copy.9 = bf16[1,64,8192]{1,0,2:T(2,128)(2,1)} copy(bf16[1,64,8192]{2,1,0:T(8,128)(2,1)} %param.3) | data formatting | bytes 2097152 | tf_op args[0]
  16.9 45.2 %reduce = bf16[8192,64]{1,0:T(8,128)(2,1)S(1)} reduce(bf16[8192,1,64]{2,1,0:T(2,128)(2,1)} %bitcast.21, bf16[]{:T(256)} %broadcast.12), dimensions={1}, to_apply=%bitcast.11.reduce_sub_computation | reduce | bytes 2097154
  62.1 1.5 reshape.14
  63.6 19.1 %all_to_all.15 = bf16[16,2,16384]{2,1,0:T(2,128)(2,1)S(1)} all-to-all(bf16[16,2,16384]{2,1,0:T(2,128)(2,1)S(1)} %reshape.14), channel_id=1, replica_groups=mesh['section'=16,'tensor'=16] {'section'}, dimensions={0} | all-to-all | bytes 2097152 | tf_op jit(solution)/shard_map/all_to_all | solution.py:18
  82.7 7.0 %reshape.15 = bf16[8192,1,64]{2,1,0:T(2,128)(2,1)} reshape(bf16[16,2,16384]{2,1,0:T(2,128)(2,1)S(1)} %all_to_all.15) | data formatting | bytes 2097152
  89.7 8.2 %copy.10 = bf16[1,64,8192]{2,1,0:T(8,128)(2,1)S(1)} copy(bf16[1,64,8192]{1,0,2:T(2,128)(2,1)} %bitcast.22) | data formatting | bytes 2097152 | tf_op jit(solution)/shard_map/all_to_all | solution.py:18
  98.3 0.6 copy.11
  98.9 1.2 copy-done.2
  100.0 8.1 %fusion.2 = f32[1024,4096]{1,0:T(8,128)} fusion(bf16[1024,512]{1,0:T(8,128)(2,1)S(1)} %bitcast.25, bf16[512,4096]{1,0:T(8,128)(2,1)S(1)} %copy-done.2), kind=kOutput, calls=%fused_computation.13 | convolution fusion | flops 4294967296 | bytes 22020096 | tf_op jit(solution)/shard_map/dot_general | solution.py:21
  108.2 100.5 %reduce-scatter.3.cloned.1.call-done = f32[64,4096]{1,0:T(8,128)} async-done(((f32[1024,4096]{1,0:T(8,128)}), f32[64,4096]{1,0:T(8,128)}) %reduce-scatter.3.cloned.1.call-update) | async-done | bytes 1048592 | tf_op jit(solution)/shard_map/reduce_scatter | solution.py:20
  208.6 2.5 fusion.1
  211.8 122.8 %all-reduce.4.cloned.1.call-done = f32[64,4096]{1,0:T(8,128)} async-done(((f32[64,4096]{1,0:T(8,128)}), f32[64,4096]{1,0:T(8,128)}) %all-reduce.4.cloned.1.call-update) | async-done | bytes 1048592 | tf_op jit(solution)/shard_map/psum | solution.py:11
  334.6 1.5 multiply_reduce_fusion.1
  336.1 45.0 %all-reduce.1 = (f32[64]{0:T(128)S(1)}, f32[64]{0:T(128)S(1)}) all-reduce(f32[64]{0:T(128)S(1)} %multiply_reduce_fusion.1, f32[64]{0:T(128)S(1)} %get-tuple-element.14), channel_id=1, replica_groups=mesh['section'=16,'tensor'=16] {'tensor'}, use_global_device_ids=true, to_apply=%region_7.8 | all-reduce | flops 128 | bytes 1024 | tf_op jit(solution)/shard_map/pmax | solution.py:30
  381.1 1.7 exponential_reduce_fusion
  382.8 39.2 %all-reduce = (f32[64]{0:T(128)S(1)}, f32[64]{0:T(128)S(1)}) all-reduce(f32[64]{0:T(128)S(1)} %get-tuple-element.16, f32[64]{0:T(128)S(1)} %get-tuple-element.17), channel_id=1, replica_groups=mesh['section'=16,'tensor'=16] {'tensor'}, use_global_device_ids=true, to_apply=%region_9.10 | all-reduce | flops 128 | bytes 1024 | tf_op jit(solution)/shard_map/psum | solution.py:31
  422.1 2.4 multiply_reduce_fusion
  424.4 42.0 %psum.31 = f32[64]{0:T(128)S(1)} all-reduce(f32[64]{0:T(128)S(1)} %multiply_reduce_fusion), channel_id=1, replica_groups=mesh['section'=16,'tensor'=16] {'tensor'}, use_global_device_ids=true, to_apply=%region_11.12 | all-reduce | flops 64 | bytes 512 | tf_op jit(solution)/shard_map/psum | solution.py:45
  466.4 1.9 multiply_convert_fusion
  468.4 49.5 %all-gather.2.cloned.1.call-done = bf16[1024,4096]{1,0:T(8,128)(2,1)} async-done(((bf16[64,4096]{1,0:T(8,128)(2,1)}), bf16[1024,4096]{1,0:T(8,128)(2,1)}) %all-gather.2.cloned.1.call-update) | async-done | bytes 8388624 | tf_op jit(solution)/shard_map/all_gather | solution.py:49
  517.9 10.5 %fusion.3 = f32[1024,512]{1,0:T(8,128)} fusion(bf16[1024,4096]{1,0:T(8,128)(2,1)} %all-gather.2.cloned.1.call-done, bf16[512,4096]{1,0:T(8,128)(2,1)} %param.4), kind=kOutput, calls=%fused_computation.14 | convolution fusion | flops 4294967296 | bytes 14680064 | tf_op jit(solution)/shard_map/dot_general | solution.py:53
  528.4 9.8 %fusion = bf16[512,4096]{0,1:T(8,128)(2,1)} fusion(bf16[1024,4096]{1,0:T(8,128)(2,1)} %all-gather.2.cloned.1.call-done, bf16[1024,512]{1,0:T(8,128)(2,1)S(1)} %bitcast.26), kind=kOutput, calls=%fused_computation.1 | convolution fusion | flops 4297064448 | bytes 13631488 | tf_op jit(solution)/shard_map/dot_general | solution.py:50
  538.1 6.3 %copy.12 = bf16[512,4096]{1,0:T(8,128)(2,1)} copy(bf16[512,4096]{0,1:T(8,128)(2,1)} %fusion) | data formatting | bytes 8388608
  544.4 73.9 %reduce-scatter.5.cloned.1.call-done = f32[64,512]{1,0:T(8,128)} async-done(((f32[1024,512]{1,0:T(8,128)}), f32[64,512]{1,0:T(8,128)}) %reduce-scatter.5.cloned.1.call-update) | async-done | bytes 131088 | tf_op jit(solution)/shard_map/reduce_scatter | solution.py:58
  (18 shorter events, 1.2 us)
Async XLA Ops:
  7.2 201.4 %reduce-scatter.3.cloned.1.call-start = ((), (), s32[]{:S(2)}) async-start(), calls=%async_computation.3 | async-start | bytes 17825792 | tf_op jit(solution)/shard_map/reduce_scatter | solution.py:20
  97.8 2.2 copy-start.2
  108.1 226.5 %all-reduce.4.cloned.1.call-start = ((), (), s32[]{:S(2)}) async-start(), calls=%async_computation.4 | async-start | bytes 2097152 | tf_op jit(solution)/shard_map/psum | solution.py:11
  208.6 172.5 %copy-start.1 = (f32[64,4096]{1,0:T(8,128)S(1)}, f32[64,4096]{1,0:T(8,128)}, u32[]{:S(2)}) copy-start(f32[64,4096]{1,0:T(8,128)} %reduce-scatter.3.cloned.1.call-done) | copy-start | bytes 3145732
  211.1 306.8 %all-gather.2.cloned.1.call-start = ((), (), s32[]{:S(2)}) async-start(), calls=%async_computation.5 | async-start | bytes 8912896 | tf_op jit(solution)/shard_map/all_gather | solution.py:49
  334.6 131.8 %copy-start = (f32[64,4096]{1,0:T(8,128)S(1)}, f32[64,4096]{1,0:T(8,128)}, u32[]{:S(2)}) copy-start(f32[64,4096]{1,0:T(8,128)} %all-reduce.4.cloned.1.call-done) | copy-start | bytes 3145732
  468.3 150.0 %reduce-scatter.5.cloned.1.call-start = ((), (), s32[]{:S(2)}) async-start(), calls=%async_computation.6 | async-start | bytes 2228224 | tf_op jit(solution)/shard_map/reduce_scatter | solution.py:58
Sparse Core Ops, SparseCore 0:
  108.2 100.3 reduce-scatter.2
  211.8 122.7 all-reduce.3
  468.5 49.3 all-gather.1
  528.5 89.8 reduce-scatter.4
where the time goes:
time: 626 us; the launch traced here: 625 us
  waiting for transfers between devices  347 us (55%)
  blocking collectives  145 us (23%)
  other arithmetic  55.1 us (9%)
  local copies, waits for them, and re-layouts  34.7 us (6%)
  matrix products  28.3 us (5%)
  between operations  14.5 us (2%)
    psum x1, waiting for transfers between devices, from_root(): return lax.psum(kept, axis)  123 us
    reduce_scatter x1, waiting for transfers between devices, local(): lax.psum_scatter(jnp.dot(flat_hidden, head, preferred_element_type=jnp.fl...  100 us
    reduce_scatter x1, waiting for transfers between devices, local(): lax.psum_scatter(hidden_part, 'tensor', scatter_dimension=0, tiled=True)  73.9 us
    all_gather x1, waiting for transfers between devices, local(): piece = lax.all_gather(grad_logits, 'section', axis=0, tiled=True)  49.5 us
    unnamed x1, other arithmetic  45.2 us
    pmax x1, blocking collectives, local(): student_max, teacher_max = lax.pmax((local_smax, local_tmax), 'tensor')  45 us
    psum x1, blocking collectives, local(): average = lax.psum(jnp.sum(student * midpoint_difference, axis=1), 'tensor')  42 us
    psum x1, blocking collectives, local(): lax.psum((jnp.sum(jnp.exp(own_logits - student_max[:, None]), axis=1), jn...  39.2 us
  transfers between devices with their start and end apart: 4, of which 4 were waited for; matrix products, arithmetic and copies ran while one was open for 3% of the time, Pallas kernels for 0%

commit v1 on v0

--- a/solution.py
+++ b/solution.py
@@ -15,7 +15,12 @@
     departure_number = lax.axis_size("section")
     tok_count = hidden.shape[1]
     row_count = departure_number * tok_count
-    local_cols = lax.all_to_all(hidden, "section", split_axis=2, concat_axis=0, tiled=True)
+    local_cols = jnp.concatenate(
+        lax.all_to_all(
+            jnp.stack(jnp.split(hidden, lax.axis_size("section"), axis=2)), "section", 0, 0
+        ),
+        axis=0,
+    )
     flat_hidden = local_cols.reshape(row_count, local_cols.shape[2])
     own_logits = lax.psum_scatter(
         jnp.dot(flat_hidden, head, preferred_element_type=jnp.float32),

time: 626 us -> 566 us (0.904)
  other arithmetic: 55.1 us -> 9.88 us
  local copies, waits for them, and re-layouts: 34.7 us -> 13.9 us
    unnamed x1 -> x0, other arithmetic: 45.2 us -> none
    unnamed x12 -> x21, local copies, waits for them, and re-layouts: 25.9 us -> 13.1 us
    all_to_all x3 -> x0, local copies, waits for them, and re-layouts: 8.81 us -> none  [local(): lax.all_to_all(hidden, 'section', split_axis=2, concat_axis=0, tiled=True)]
    reduce_scatter x1, waiting for transfers between devices: 73.9 us -> 80.3 us  [local(): lax.psum_scatter(hidden_part, 'tensor', scatter_dimension=0, tiled=True)]
  transfers between devices with their start and end apart: 4 -> 4, of which waited for: 4 -> 4; matrix products, arithmetic and copies ran while one was open for 3% -> 2% of each run, Pallas kernels for 0% -> 0%
where the time goes in v1:
time: 566 us; the launch traced here: 565 us
  waiting for transfers between devices  353 us (62%)
  blocking collectives  145 us (26%)
  matrix products  28 us (5%)
  between operations  14.5 us (3%)
  local copies, waits for them, and re-layouts  13.9 us (2%)
  other arithmetic  9.88 us (2%)
    psum x1, waiting for transfers between devices, from_root(): return lax.psum(kept, axis)  123 us
    reduce_scatter x1, waiting for transfers between devices, local(): lax.psum_scatter(jnp.dot(flat_hidden, head, preferred_element_type=jnp.fl...  100 us
    reduce_scatter x1, waiting for transfers between devices, local(): lax.psum_scatter(hidden_part, 'tensor', scatter_dimension=0, tiled=True)  80.3 us
    all_gather x1, waiting for transfers between devices, local(): piece = lax.all_gather(grad_logits, 'section', axis=0, tiled=True)  49.5 us
    pmax x1, blocking collectives, local(): student_max, teacher_max = lax.pmax((local_smax, local_tmax), 'tensor')  45 us
    psum x1, blocking collectives, local(): average = lax.psum(jnp.sum(student * midpoint_difference, axis=1), 'tensor')  42 us
    psum x1, blocking collectives, local(): lax.psum((jnp.sum(jnp.exp(own_logits - student_max[:, None]), axis=1), jn...  39.1 us
    all_to_all x1, blocking collectives, local(): lax.all_to_all(jnp.stack(jnp.split(hidden, lax.axis_size('section'), axis...  19.1 us
  transfers between devices with their start and end apart: 4, of which 4 were waited for; matrix products, arithmetic and copies ran while one was open for 2% of the time, Pallas kernels for 0%

profile of v1, /device:TPU:8, one launch (start us, length us, event | category | flops | bytes accessed | tf_op | source)
XLA Modules:
  0.0 564.8 jit_solution(17445542676295770635)
XLA Ops:
  7.2 1.0 bitcast_dynamic-update-slice_fusion.15
  8.2 1.1 bitcast_dynamic-update-slice_fusion.14
  9.3 0.8 bitcast_dynamic-update-slice_fusion.13
  10.2 0.8 bitcast_dynamic-update-slice_fusion.12
  11.8 0.8 bitcast_dynamic-update-slice_fusion.10
  13.5 0.8 bitcast_dynamic-update-slice_fusion.8
  15.2 0.8 bitcast_dynamic-update-slice_fusion.6
  16.9 0.8 bitcast_dynamic-update-slice_fusion.4
  21.1 19.1 %all_to_all.5 = bf16[16,1,64,512]{3,2,1,0:T(8,128)(2,1)S(1)} all-to-all(bf16[16,1,64,512]{3,2,1,0:T(8,128)(2,1)S(1)} %bitcast_dynamic-update-slice_fusion), channel_id=1, replica_groups=mesh['section'=16,'tensor'=16] {'section'}, dimensions={0} | all-to-all | bytes 2097152 | tf_op jit(solution)/shard_map/all_to_all | solution.py:19
  40.3 8.1 %fusion.1 = f32[1024,4096]{1,0:T(8,128)} fusion(bf16[1024,512]{1,0:T(8,128)(2,1)S(1)} %bitcast.41, bf16[512,4096]{1,0:T(8,128)(2,1)S(1)} %copy-done.2), kind=kOutput, calls=%fused_computation.27 | convolution fusion | flops 4294967296 | bytes 22020096 | tf_op jit(solution)/shard_map/dot_general | solution.py:26
  48.4 100.5 %reduce-scatter.3.cloned.1.call-done = f32[64,4096]{1,0:T(8,128)} async-done(((f32[1024,4096]{1,0:T(8,128)}), f32[64,4096]{1,0:T(8,128)}) %reduce-scatter.3.cloned.1.call-update) | async-done | bytes 1048592 | tf_op jit(solution)/shard_map/reduce_scatter | solution.py:25
  148.9 2.5 fusion
  152.0 122.8 %all-reduce.4.cloned.1.call-done = f32[64,4096]{1,0:T(8,128)} async-done(((f32[64,4096]{1,0:T(8,128)}), f32[64,4096]{1,0:T(8,128)}) %all-reduce.4.cloned.1.call-update) | async-done | bytes 1048592 | tf_op jit(solution)/shard_map/psum | solution.py:11
  274.8 1.5 multiply_reduce_fusion.1
  276.3 45.0 %all-reduce.1 = (f32[64]{0:T(128)S(1)}, f32[64]{0:T(128)S(1)}) all-reduce(f32[64]{0:T(128)S(1)} %multiply_reduce_fusion.1, f32[64]{0:T(128)S(1)} %get-tuple-element.6), channel_id=1, replica_groups=mesh['section'=16,'tensor'=16] {'tensor'}, use_global_device_ids=true, to_apply=%region_7.8 | all-reduce | flops 128 | bytes 1024 | tf_op jit(solution)/shard_map/pmax | solution.py:35
  321.4 1.7 exponential_reduce_fusion
  323.1 39.1 %all-reduce = (f32[64]{0:T(128)S(1)}, f32[64]{0:T(128)S(1)}) all-reduce(f32[64]{0:T(128)S(1)} %get-tuple-element.8, f32[64]{0:T(128)S(1)} %get-tuple-element.9), channel_id=1, replica_groups=mesh['section'=16,'tensor'=16] {'tensor'}, use_global_device_ids=true, to_apply=%region_9.10 | all-reduce | flops 128 | bytes 1024 | tf_op jit(solution)/shard_map/psum | solution.py:36
  362.1 2.4 multiply_reduce_fusion
  364.5 42.0 %psum.31 = f32[64]{0:T(128)S(1)} all-reduce(f32[64]{0:T(128)S(1)} %multiply_reduce_fusion), channel_id=1, replica_groups=mesh['section'=16,'tensor'=16] {'tensor'}, use_global_device_ids=true, to_apply=%region_11.12 | all-reduce | flops 64 | bytes 512 | tf_op jit(solution)/shard_map/psum | solution.py:50
  406.5 1.9 multiply_convert_fusion
  408.4 49.5 %all-gather.2.cloned.1.call-done = bf16[1024,4096]{1,0:T(8,128)(2,1)} async-done(((bf16[64,4096]{1,0:T(8,128)(2,1)}), bf16[1024,4096]{1,0:T(8,128)(2,1)}) %all-gather.2.cloned.1.call-update) | async-done | bytes 8388624 | tf_op jit(solution)/shard_map/all_gather | solution.py:54
  457.9 10.5 %fusion.2 = f32[1024,512]{1,0:T(8,128)} fusion(bf16[1024,4096]{1,0:T(8,128)(2,1)} %all-gather.2.cloned.1.call-done, bf16[512,4096]{1,0:T(8,128)(2,1)} %param.4), kind=kOutput, calls=%fused_computation.28 | convolution fusion | flops 4294967296 | bytes 14680064 | tf_op jit(solution)/shard_map/dot_general | solution.py:58
  468.4 9.5 %convolution_convert_fusion = bf16[512,4096]{1,0:T(8,128)(2,1)} fusion(bf16[1024,512]{1,0:T(8,128)(2,1)S(1)} %bitcast.42, bf16[1024,4096]{1,0:T(8,128)(2,1)} %all-gather.2.cloned.1.call-done), kind=kOutput, calls=%fused_computation | convolution fusion | flops 4297064448 | bytes 13631488 | tf_op jit(solution)/shard_map/dot_general | solution.py:55
  478.0 80.3 %reduce-scatter.5.cloned.1.call-done = f32[64,512]{1,0:T(8,128)} async-done(((f32[1024,512]{1,0:T(8,128)}), f32[64,512]{1,0:T(8,128)}) %reduce-scatter.5.cloned.1.call-update) | async-done | bytes 131088 | tf_op jit(solution)/shard_map/reduce_scatter | solution.py:63
  (24 shorter events, 7.0 us)
Async XLA Ops:
  7.2 141.7 %reduce-scatter.3.cloned.1.call-start = ((), (), s32[]{:S(2)}) async-start(), calls=%async_computation.3 | async-start | bytes 17825792 | tf_op jit(solution)/shard_map/reduce_scatter | solution.py:25
  7.2 33.0 %copy-start.2 = (bf16[512,4096]{1,0:T(8,128)(2,1)S(1)}, bf16[512,4096]{1,0:T(8,128)(2,1)}, u32[]{:S(2)}) copy-start(bf16[512,4096]{1,0:T(8,128)(2,1)} %param.4) | copy-start | bytes 12582916
  48.3 226.5 %all-reduce.4.cloned.1.call-start = ((), (), s32[]{:S(2)}) async-start(), calls=%async_computation.4 | async-start | bytes 2097152 | tf_op jit(solution)/shard_map/psum | solution.py:11
  148.9 172.5 %copy-start.1 = (f32[64,4096]{1,0:T(8,128)S(1)}, f32[64,4096]{1,0:T(8,128)}, u32[]{:S(2)}) copy-start(f32[64,4096]{1,0:T(8,128)} %reduce-scatter.3.cloned.1.call-done) | copy-start | bytes 3145732
  151.3 306.6 %all-gather.2.cloned.1.call-start = ((), (), s32[]{:S(2)}) async-start(), calls=%async_computation.5 | async-start | bytes 8912896 | tf_op jit(solution)/shard_map/all_gather | solution.py:54
  274.8 131.7 %copy-start = (f32[64,4096]{1,0:T(8,128)S(1)}, f32[64,4096]{1,0:T(8,128)}, u32[]{:S(2)}) copy-start(f32[64,4096]{1,0:T(8,128)} %all-reduce.4.cloned.1.call-done) | copy-start | bytes 3145732
  408.4 149.9 %reduce-scatter.5.cloned.1.call-start = ((), (), s32[]{:S(2)}) async-start(), calls=%async_computation.6 | async-start | bytes 2228224 | tf_op jit(solution)/shard_map/reduce_scatter | solution.py:63
Sparse Core Ops, SparseCore 0:
  48.5 100.3 reduce-scatter.2
  152.1 122.7 all-reduce.3
  408.5 49.3 all-gather.1
  468.6 89.6 reduce-scatter.4
